TPU v7x, 32 devices: a whole 2x2x4 slice. The times are simulated.
32 devices in a mesh: src: 8 (over z, core), rcv: 4 (over y, x).
Axes of the slice: x: 2, y: 2, z: 4, core: 2. Of those that a mesh axis runs over, the one named last changes fastest.
Arguments:
- spectra: bfloat16 [128, 4, 2, 2048], P(('src', 'rcv')), may hold values from -50 to 50
- valid: int32 [128, 4], P(('src', 'rcv')), may hold values 0 or 1
Outputs:
- correlations: bfloat16 [128, 128, 512], P('src', 'rcv')
All inputs are finite; a program needn't handle non-finite values. No bound on the sum of `valid` on one device may be relied on, other than what follows from the above.
Results may differ from a plain program's by a relative error of at most 0.0065.
Values may be sent and summed in bfloat16 or wider, within the bound.
No kernel may reach another device: no remote copies, remote signals or barrier semaphores. Data moves between devices by JAX's collectives and lax.ppermute only.
A program may use at most 64 MiB of HBM per device.

v0:
```python
import math
import jax
import jax.numpy as jnp
from jax import lax
from jax.sharding import PartitionSpec as P

LAGS = 512
BAND = 32
NSAMP = 7500
epsilon = 1e-06


def whiten_spectra(spectra):
    values = spectra.astype(jnp.float32)
    squares = values[:, :, 0] ** 2 + values[:, :, 1] ** 2
    banded = squares.reshape(squares.shape[0], squares.shape[1], squares.shape[2] // BAND, BAND)
    power = jnp.sum(banded, axis=3) / (2.0 * BAND)
    factor = jnp.repeat(1.0 / jnp.sqrt(power + epsilon), BAND, axis=2)
    return (values * factor[:, :, None, :]).astype(jnp.bfloat16)


def lag_table(freq_count, lag_count):
    bins_index = jnp.arange(freq_count, dtype=jnp.int32)
    shifts = jnp.arange(lag_count, dtype=jnp.int32) - lag_count // 2
    phase = jnp.mod(bins_index[:, None] * shifts[None, :], NSAMP)
    angle = phase.astype(jnp.float32) * (2.0 * math.pi / NSAMP)
    factor = 1.0 / math.sqrt(2.0 * freq_count)
    cosines = (jnp.cos(angle) * factor).astype(jnp.bfloat16)
    sines = (-jnp.sin(angle) * factor).astype(jnp.bfloat16)
    return jnp.concatenate([cosines, sines], axis=0)


def weighted_cross(rec_spec, rec_mask, src_spec, src_mask):
    counts = jnp.dot(rec_mask, src_mask.T, preferred_element_type=jnp.float32)
    inverse = 1.0 / jnp.maximum(counts, 1.0)
    real_part = jnp.zeros((rec_spec.shape[0], src_spec.shape[0], rec_spec.shape[-1]), jnp.float32)
    imag_part = jnp.zeros_like(real_part)
    for window in range(rec_spec.shape[1]):
        rec_a = rec_spec[:, window, 0].astype(jnp.float32)[:, None, :]
        rec_b = rec_spec[:, window, 1].astype(jnp.float32)[:, None, :]
        src_a = src_spec[:, window, 0].astype(jnp.float32)[None, :, :]
        src_b = src_spec[:, window, 1].astype(jnp.float32)[None, :, :]
        pair_weight = (rec_mask[:, window][:, None] * src_mask[:, window][None, :] * inverse)[
            :, :, None
        ]
        real_part = real_part + pair_weight * (src_a * rec_a + src_b * rec_b)
        imag_part = imag_part + pair_weight * (src_b * rec_a - src_a * rec_b)
    return (real_part, imag_part)


def correlate_block(rec_spec, rec_mask, src_spec, src_mask, table):
    real_part, imag_part = weighted_cross(rec_spec, rec_mask, src_spec, src_mask)
    stacked = jnp.concatenate(
        [real_part.astype(jnp.bfloat16), imag_part.astype(jnp.bfloat16)], axis=2
    )
    return jnp.einsum("iqk,kl->iql", stacked, table, preferred_element_type=jnp.float32)


def group_rows(rec_spec, rec_mask, src_spec, src_mask, table):
    receiver_count = rec_spec.shape[0]
    group_count = receiver_count // 8
    source_masks = src_mask.astype(jnp.float32)

    def one_group(group):
        return correlate_block(
            group[0], group[1].astype(jnp.float32), src_spec, source_masks, table
        ).astype(jnp.bfloat16)

    grouped = (
        rec_spec.reshape((group_count, 8) + rec_spec.shape[1:]),
        rec_mask.reshape(group_count, 8, rec_mask.shape[1]),
    )
    result = lax.map(one_group, grouped)
    return result.reshape(receiver_count, src_spec.shape[0], table.shape[1])


def local(spectra, valid):
    table = lag_table(spectra.shape[-1], LAGS)
    mask_wire = valid.astype(jnp.bfloat16)
    whitened = whiten_spectra(spectra)
    rec_spec, rec_mask = (
        lax.all_gather(whitened, "rcv", axis=0, tiled=True),
        lax.all_gather(mask_wire, "rcv", axis=0, tiled=True),
    )
    portion = lax.all_gather((whitened, mask_wire), "src", axis=0, tiled=True)
    return group_rows(rec_spec, rec_mask, portion[0], portion[1], table)


def solution(mesh):
    return jax.shard_map(
        local,
        mesh=mesh,
        in_specs=(P(("src", "rcv"), None, None, None), P(("src", "rcv"), None)),
        out_specs=P("src", "rcv", None),
        check_vma=False,
    )
```

profile of v0, /device:TPU:0, one launch (start us, length us, event | category | flops | bytes accessed | tf_op | source)
XLA Modules:
  0.0 84.7 jit_solution(15054777667643042789)
XLA Ops:
  6.5 0.0 copy-start.1
  6.5 0.0 copy-start.2
  6.5 0.0 all-gather.4.cloned.1.call-start
  6.5 1.0 %copy_convert_fusion = f32[4,4,2,2048]{3,1,2,0:T(4,128)S(1)} fusion(bf16[4,4,2,2048]{3,2,1,0:T(2,128)(2,1)} %param.4), kind=kLoop, calls=%fused_computation.68 | loop fusion | flops 65536 | bytes 393216 | tf_op jit(solution)/shard_map/convert_element_type | solution.py:14
  7.6 0.2 add.64
  7.8 0.2 reduce_sum.9
  8.0 0.2 broadcast_in_dim.8
  8.3 0.3 mul.164
  8.5 0.0 copy-done.1
  8.5 0.7 multiply_convert_fusion.2
  9.3 0.0 all-gather.4.cloned.1.call-update
  9.3 0.0 copy-done.2
  9.3 9.5 %all-gather = bf16[4,4,4]{2,1,0:T(4,128)(2,1)S(1)} all-gather(bf16[1,4,4]{2,1,0:T(4,128)(2,1)S(1)} %convert_bitcast_fusion), channel_id=1, replica_groups=mesh['src'=8,'rcv'=4] {'rcv'}, dimensions={0}, use_global_device_ids=true | all-gather | bytes 160 | tf_op jit(solution)/shard_map/all_gather | solution.py:83
  18.8 12.0 %all-gather.1 = bf16[8,4,4]{2,1,0:T(4,128)(2,1)S(1)} all-gather(bf16[1,4,4]{2,1,0:T(4,128)(2,1)S(1)} %convert_bitcast_fusion), channel_id=1, replica_groups=mesh['src'=8,'rcv'=4] {'src'}, dimensions={0}, use_global_device_ids=true | all-gather | bytes 288 | tf_op jit(solution)/shard_map/all_gather | solution.py:85
  30.9 0.1 copy.22
  31.0 0.1 copy.23
  31.1 0.1 reshape.163
  31.2 0.1 copy.26
  31.3 10.3 %all_gather.15 = bf16[16,4,2,2048]{3,1,2,0:T(4,128)(2,1)S(1)} all-gather(bf16[4,4,2,2048]{3,1,2,0:T(4,128)(2,1)} %multiply_convert_fusion.2), channel_id=1, replica_groups=mesh['src'=8,'rcv'=4] {'rcv'}, dimensions={0}, use_global_device_ids=true | all-gather | bytes 655360 | tf_op jit(solution)/shard_map/all_gather | solution.py:82
  41.5 17.7 %multiply_convert_fusion.1 = (bf16[2048,512]{1,0:T(8,128)(2,1)S(1)}, bf16[2048,512]{1,0:T(8,128)(2,1)S(1)}) fusion(s32[512]{0:T(512)S(1)} %iota_add_fusion), kind=kLoop, calls=%fused_computation.59 | loop fusion | flops 14680064 | bytes 4196352 | tf_op jit(solution)/shard_map/convert_element_type | solution.py:28
  59.2 2.2 %pad_maximum_fusion = bf16[4096,512]{1,0:T(8,128)(2,1)} fusion(bf16[2048,512]{1,0:T(8,128)(2,1)S(1)} %get-tuple-element.114, bf16[2048,512]{1,0:T(8,128)(2,1)S(1)} %get-tuple-element.113), kind=kLoop, calls=%fused_computation.57 | loop fusion | flops 8388608 | bytes 8388608 | tf_op jit(solution)/shard_map/concatenate | solution.py:30
  61.4 0.0 all-gather.4.cloned.1.call-done
  61.4 1.8 %copy.27 = bf16[32,4,2,2048]{3,0,2,1:T(8,128)(2,1)S(1)} copy(bf16[32,4,2,2048]{3,1,2,0:T(4,128)(2,1)} %all-gather.4.cloned.1.call-done) | data formatting | bytes 2097152 | tf_op jit(solution)/shard_map/while | solution.py:73
  63.2 13.8 %while.10 = (s32[]{:T(128)}, bf16[2,8,32,512]{3,2,1,0:T(8,128)(2,1)S(1)}, bf16[2,8,4]{1,2,0:T(4,128)(2,1)S(1)}, f32[32,4]{0,1:T(4,128)S(1)}, bf16[32,4,2,2048]{3...) while((s32[]{:T(128)}, ...), condition=%wide.region_2.3_spmd, body=%wide.region_1.2_spmd.sunk | while | flops 1099698688 | bytes 35672640 | solution.py:73
  63.3 0.2 multiply_multiply_fusion.5
  63.5 0.1 constant_dynamic-slice_fusion.4
  63.6 0.2 copy.40
  63.8 0.2 bitcast_convert_fusion.11
  64.1 0.0 copy-start
  64.1 2.3 %add_convert_fusion.5 = bf16[8,32,2048]{2,1,0:T(8,128)(2,1)S(1)} fusion(f32[8,2048]{1,0:T(8,128)S(1)} %get-tuple-element.186, f32[32,2048]{1,0:T(8,128)S(1)} %get-tuple-element.187, f32[8,2048]{1,0:T(8,128)S(1)} %get-tuple-element.188, f32[32,2048]{1,0:T(8,128)S(1)} %get-tuple-element.189, f32[8,32]{1,0:T(8,128)S(1)} %get-tuple-element.198, ...), kind=kLoop, calls=%fused_computation.6.clone.1 | loop fusion | flops 10485760 | bytes 3674112 | tf_op jit(solution)/shard_map/while/body/eval_jaxpr/convert_element_type | solution.py:54
  66.4 2.5 %add_convert_fusion.4 = bf16[8,32,2048]{2,1,0:T(8,128)(2,1)S(1)} fusion(f32[8,2048]{1,0:T(8,128)S(1)} %get-tuple-element.186, f32[32,2048]{1,0:T(8,128)S(1)} %get-tuple-element.187, f32[8,2048]{1,0:T(8,128)S(1)} %get-tuple-element.188, f32[32,2048]{1,0:T(8,128)S(1)} %get-tuple-element.189, f32[8,32]{1,0:T(8,128)S(1)} %get-tuple-element.198, ...), kind=kLoop, calls=%fused_computation.5.clone.1 | loop fusion | flops 10485760 | bytes 3674112 | tf_op jit(solution)/shard_map/while/body/eval_jaxpr/convert_element_type | solution.py:54
  68.9 0.0 copy-done
  68.9 1.2 %fusion.47 = bf16[2,8,32,512]{3,2,1,0:T(8,128)(2,1)S(1)} fusion(bf16[2,8,32,512]{3,2,1,0:T(8,128)(2,1)S(1)} %get-tuple-element.223, s32[]{:T(128)} %get-tuple-element.222, bf16[4096,512]{1,0:T(8,128)(2,1)S(1)} %copy-done, bf16[8,32,2048]{2,1,0:T(8,128)(2,1)S(1)} %add_convert_fusion.4, bf16[8,32,2048]{2,1,0:T(8,128)(2,1)S(1)} %add_convert_fusion.5), kind=kOutput, calls=%fused_computation.9.clone.1 | convolution fusion | flops 1078067200 | bytes 6553604 | tf_op jit(solution)/shard_map/while/body/eval_jaxpr/iqk,kl->iql/dot_general | solution.py:56
  70.2 0.2 multiply_multiply_fusion.5
  70.4 0.1 constant_dynamic-slice_fusion.4
  70.5 0.2 copy.40
  70.7 0.2 bitcast_convert_fusion.11
  70.9 0.0 copy-start
  71.0 2.3 %add_convert_fusion.5 = bf16[8,32,2048]{2,1,0:T(8,128)(2,1)S(1)} fusion(f32[8,2048]{1,0:T(8,128)S(1)} %get-tuple-element.186, f32[32,2048]{1,0:T(8,128)S(1)} %get-tuple-element.187, f32[8,2048]{1,0:T(8,128)S(1)} %get-tuple-element.188, f32[32,2048]{1,0:T(8,128)S(1)} %get-tuple-element.189, f32[8,32]{1,0:T(8,128)S(1)} %get-tuple-element.198, ...), kind=kLoop, calls=%fused_computation.6.clone.1 | loop fusion | flops 10485760 | bytes 3674112 | tf_op jit(solution)/shard_map/while/body/eval_jaxpr/convert_element_type | solution.py:54
  73.3 2.5 %add_convert_fusion.4 = bf16[8,32,2048]{2,1,0:T(8,128)(2,1)S(1)} fusion(f32[8,2048]{1,0:T(8,128)S(1)} %get-tuple-element.186, f32[32,2048]{1,0:T(8,128)S(1)} %get-tuple-element.187, f32[8,2048]{1,0:T(8,128)S(1)} %get-tuple-element.188, f32[32,2048]{1,0:T(8,128)S(1)} %get-tuple-element.189, f32[8,32]{1,0:T(8,128)S(1)} %get-tuple-element.198, ...), kind=kLoop, calls=%fused_computation.5.clone.1 | loop fusion | flops 10485760 | bytes 3674112 | tf_op jit(solution)/shard_map/while/body/eval_jaxpr/convert_element_type | solution.py:54
  75.8 0.0 copy-done
  75.8 1.2 %fusion.47 = bf16[2,8,32,512]{3,2,1,0:T(8,128)(2,1)S(1)} fusion(bf16[2,8,32,512]{3,2,1,0:T(8,128)(2,1)S(1)} %get-tuple-element.223, s32[]{:T(128)} %get-tuple-element.222, bf16[4096,512]{1,0:T(8,128)(2,1)S(1)} %copy-done, bf16[8,32,2048]{2,1,0:T(8,128)(2,1)S(1)} %add_convert_fusion.4, bf16[8,32,2048]{2,1,0:T(8,128)(2,1)S(1)} %add_convert_fusion.5), kind=kOutput, calls=%fused_computation.9.clone.1 | convolution fusion | flops 1078067200 | bytes 6553604 | tf_op jit(solution)/shard_map/while/body/eval_jaxpr/iqk,kl->iql/dot_general | solution.py:56
  77.0 0.0 copy-start.3
  77.0 0.8 copy-done.3
  (13 shorter events, 0.2 us)
Async XLA Ops:
  6.5 2.0 %copy-start.1 = (bf16[4,4,2,2048]{3,2,1,0:T(2,128)(2,1)S(1)}, bf16[4,4,2,2048]{3,2,1,0:T(2,128)(2,1)}, u32[]{:S(2)}) copy-start(bf16[4,4,2,2048]{3,2,1,0:T(2,128)(2,1)} %param.4) | copy-start | bytes 393220
  6.5 2.8 %copy-start.2 = (s32[4,4]{1,0:T(4,128)S(1)}, s32[4,4]{1,0:T(4,128)}, u32[]{:S(2)}) copy-start(s32[4,4]{1,0:T(4,128)} %param.5) | copy-start | bytes 196
  6.5 54.9 %all-gather.4.cloned.1.call-start = ((), (), s32[]{:S(2)}) async-start(), calls=%async_computation | async-start | bytes 1179648 | tf_op jit(solution)/shard_map/all_gather | solution.py:85
  64.1 4.8 %copy-start = (bf16[4096,512]{1,0:T(8,128)(2,1)S(1)}, bf16[4096,512]{1,0:T(8,128)(2,1)}, u32[]{:S(2)}) copy-start(bf16[4096,512]{1,0:T(8,128)(2,1)} %get-tuple-element.236) | copy-start | bytes 12582916 | tf_op jit(solution)/shard_map/while
  70.9 4.8 %copy-start = (bf16[4096,512]{1,0:T(8,128)(2,1)S(1)}, bf16[4096,512]{1,0:T(8,128)(2,1)}, u32[]{:S(2)}) copy-start(bf16[4096,512]{1,0:T(8,128)(2,1)} %get-tuple-element.236) | copy-start | bytes 12582916 | tf_op jit(solution)/shard_map/while
  77.0 0.8 copy-start.3
Sparse Core Ops, SparseCore 0:
  9.4 24.8 all-gather.3
where the time goes:
time: 84.9 us; the launch traced here: 84.7 us
  other arithmetic  32.1 us (38%)
  blocking collectives  31.8 us (37%)
  between operations  13.5 us (16%)
  local copies, waits for them, and re-layouts  4.24 us (5%)
  matrix products  2.84 us (3%)
    convert_element_type x1, other arithmetic, lag_table(): cosines = (jnp.cos(angle) * factor).astype(jnp.bfloat16)  17.7 us
    all_gather x1, blocking collectives, local(): portion = lax.all_gather((whitened, mask_wire), 'src', axis=0, tiled=True)  12 us
    all_gather x1, blocking collectives, local(): lax.all_gather(whitened, 'rcv', axis=0, tiled=True)  10.3 us
    all_gather x1, blocking collectives, local(): lax.all_gather(mask_wire, 'rcv', axis=0, tiled=True)  9.52 us
    convert_element_type x2, other arithmetic, correlate_block(): imag_part.astype(jnp.bfloat16)  4.96 us
    convert_element_type x2, other arithmetic, correlate_block(): real_part.astype(jnp.bfloat16)  4.61 us
    dot_general x2, matrix products, correlate_block(): jnp.einsum('iqk,kl->iql', stacked, table, preferred_element_type=jnp.floa...  2.49 us
    concatenate x1, other arithmetic, lag_table(): return jnp.concatenate([cosines, sines], axis=0)  2.23 us
  transfers between devices with their start and end apart: 1, of which 0 were waited for; matrix products, arithmetic and copies ran while one was open for 24% of the time, Pallas kernels for 0%

commit v1 on v0

--- a/solution.py
+++ b/solution.py
@@ -8,6 +8,18 @@
 BAND = 32
 NSAMP = 7500
 epsilon = 1e-06
+
+
+def gather_by_bits(array, axis, dim):
+    ways, here = (lax.axis_size(axis), lax.axis_index(axis))
+    grown, reach = (array, 1)
+    while reach < ways:
+        theirs = lax.ppermute(grown, axis, [(d, d ^ reach) for d in range(ways)])
+        mine_first = jnp.concatenate([grown, theirs], axis=dim)
+        theirs_first = jnp.concatenate([theirs, grown], axis=dim)
+        grown = jnp.where(here & reach == 0, mine_first, theirs_first)
+        reach = 2 * reach
+    return grown
 
 
 def whiten_spectra(spectra):
@@ -79,7 +91,7 @@
     mask_wire = valid.astype(jnp.bfloat16)
     whitened = whiten_spectra(spectra)
     rec_spec, rec_mask = (
-        lax.all_gather(whitened, "rcv", axis=0, tiled=True),
+        gather_by_bits(whitened, "rcv", 0),
         lax.all_gather(mask_wire, "rcv", axis=0, tiled=True),
     )
     portion = lax.all_gather((whitened, mask_wire), "src", axis=0, tiled=True)

time: 84.9 us -> 77 us (0.907)
  blocking collectives: 31.8 us -> 19 us
  starting transfers between devices: 0.01 us -> 4.59 us
    all_gather x1 -> x0, blocking collectives: 10.3 us -> none  [local(): lax.all_gather(whitened, 'rcv', axis=0, tiled=True)]
    ppermute x0 -> x2, starting transfers between devices: none -> 4.59 us  [gather_by_bits(): theirs = lax.ppermute(grown, axis, [(d, d ^ reach) for d in range(ways)])]
    all_gather x1, blocking collectives: 9.52 us -> 7.07 us  [local(): lax.all_gather(mask_wire, 'rcv', axis=0, tiled=True)]
  transfers between devices with their start and end apart: 1 -> 3, of which waited for: 0 -> 0; matrix products, arithmetic and copies ran while one was open for 24% -> 28% of each run, Pallas kernels for 0% -> 0%
where the time goes in v1:
time: 77 us; the launch traced here: 76.8 us
  other arithmetic  31.8 us (41%)
  blocking collectives  19 us (25%)
  between operations  13.6 us (18%)
  local copies, waits for them, and re-layouts  4.7 us (6%)
  starting transfers between devices  4.59 us (6%)
  matrix products  2.84 us (4%)
    convert_element_type x1, other arithmetic, lag_table(): cosines = (jnp.cos(angle) * factor).astype(jnp.bfloat16)  17.7 us
    all_gather x1, blocking collectives, local(): portion = lax.all_gather((whitened, mask_wire), 'src', axis=0, tiled=True)  12 us
    all_gather x1, blocking collectives, local(): lax.all_gather(mask_wire, 'rcv', axis=0, tiled=True)  7.07 us
    convert_element_type x2, other arithmetic, correlate_block(): imag_part.astype(jnp.bfloat16)  4.96 us
    convert_element_type x2, other arithmetic, correlate_block(): real_part.astype(jnp.bfloat16)  4.61 us
    ppermute x2, starting transfers between devices, gather_by_bits(): theirs = lax.ppermute(grown, axis, [(d, d ^ reach) for d in range(ways)])  4.59 us
    dot_general x2, matrix products, correlate_block(): jnp.einsum('iqk,kl->iql', stacked, table, preferred_element_type=jnp.floa...  2.49 us
    concatenate x1, other arithmetic, lag_table(): return jnp.concatenate([cosines, sines], axis=0)  2.22 us
  transfers between devices with their start and end apart: 3, of which 0 were waited for; matrix products, arithmetic and copies ran while one was open for 28% of the time, Pallas kernels for 0%

profile of v1, /device:TPU:0, one launch (start us, length us, event | category | flops | bytes accessed | tf_op | source)
XLA Modules:
  0.0 76.8 jit_solution(638116735908146343)
XLA Ops:
  6.5 0.0 copy-start.1
  6.5 0.0 all-gather.4.cloned.1.call-start
  6.5 1.1 %copy_convert_fusion = f32[4,4,2,2048]{3,0,2,1:T(4,128)S(1)} fusion(bf16[4,4,2,2048]{3,2,1,0:T(2,128)(2,1)} %param.4), kind=kLoop, calls=%fused_computation.70 | loop fusion | flops 65536 | bytes 393216 | tf_op jit(solution)/shard_map/convert_element_type | solution.py:26
  7.7 0.1 copy.27
  7.8 0.2 add.64
  7.9 0.2 reduce_sum.9
  8.2 0.2 broadcast_in_dim.8
  8.4 0.3 mul.164
  8.7 0.1 copy.28
  8.7 0.0 copy-done.1
  8.8 0.1 multiply_convert_fusion.2
  8.9 3.0 %collective-permute-start = (bf16[4,4,2,2048]{3,0,2,1:T(4,128)(2,1)S(1)}, bf16[4,4,2,2048]{3,0,2,1:T(4,128)(2,1)S(1)}, u32[]{:S(2)}, u32[]{:S(2)}) collective-permute-start(bf16[4,4,2,2048]{3,0,2,1:T(4,128)(2,1)S(1)} %multiply_convert_fusion.2), channel_id=1, source_target_pairs={{0,1},{1,0},{2,3},{3,2},{4,5},{5,4},{6,7},{7,6},{8,9},{9,8},{10,11... | collective-permute-start | bytes 393224 | tf_op jit(solution)/shard_map/ppermute | solution.py:17
  11.9 0.8 copy.29
  12.6 0.0 all-gather.4.cloned.1.call-update
  12.7 0.0 copy-start.2
  12.7 17.7 %multiply_convert_fusion.1 = (bf16[2048,512]{1,0:T(8,128)(2,1)S(1)}, bf16[2048,512]{1,0:T(8,128)(2,1)S(1)}) fusion(s32[512]{0:T(512)S(1)} %iota_add_fusion), kind=kLoop, calls=%fused_computation.58 | loop fusion | flops 14680064 | bytes 4196352 | tf_op jit(solution)/shard_map/convert_element_type | solution.py:40
  30.4 0.0 copy-done.2
  30.4 0.0 collective-permute-done
  30.4 0.2 maximum_select_fusion.1
  30.6 1.6 %collective-permute-start.1 = (bf16[8,4,2,2048]{3,0,2,1:T(8,128)(2,1)S(1)}, bf16[8,4,2,2048]{3,0,2,1:T(8,128)(2,1)S(1)}, u32[]{:S(2)}, u32[]{:S(2)}) collective-permute-start(bf16[8,4,2,2048]{3,0,2,1:T(8,128)(2,1)S(1)} %maximum_select_fusion.1), channel_id=1, source_target_pairs={{0,2},{1,3},{2,0},{3,1},{4,6},{5,7},{6,4},{7,5},{8,10},{9,11},{10,... | collective-permute-start | bytes 786440 | tf_op jit(solution)/shard_map/ppermute | solution.py:17
  32.2 2.2 %pad_maximum_fusion = bf16[4096,512]{1,0:T(8,128)(2,1)} fusion(bf16[2048,512]{1,0:T(8,128)(2,1)S(1)} %get-tuple-element.114, bf16[2048,512]{1,0:T(8,128)(2,1)S(1)} %get-tuple-element.113), kind=kLoop, calls=%fused_computation.56 | loop fusion | flops 8388608 | bytes 8388608 | tf_op jit(solution)/shard_map/concatenate | solution.py:42
  34.4 7.1 %all-gather = bf16[4,4,4]{2,1,0:T(4,128)(2,1)S(1)} all-gather(bf16[1,4,4]{2,1,0:T(4,128)(2,1)S(1)} %convert_bitcast_fusion), channel_id=1, replica_groups=mesh['src'=8,'rcv'=4] {'rcv'}, dimensions={0}, use_global_device_ids=true | all-gather | bytes 160 | tf_op jit(solution)/shard_map/all_gather | solution.py:95
  41.5 12.0 %all-gather.1 = bf16[8,4,4]{2,1,0:T(4,128)(2,1)S(1)} all-gather(bf16[1,4,4]{2,1,0:T(4,128)(2,1)S(1)} %convert_bitcast_fusion), channel_id=1, replica_groups=mesh['src'=8,'rcv'=4] {'src'}, dimensions={0}, use_global_device_ids=true | all-gather | bytes 288 | tf_op jit(solution)/shard_map/all_gather | solution.py:97
  53.5 0.1 copy.24
  53.6 0.1 copy.25
  53.7 0.1 reshape.164
  53.8 0.1 copy.30
  53.9 0.0 collective-permute-done.1
  53.9 0.1 fusion.36
  54.0 0.0 all-gather.4.cloned.1.call-done
  54.0 1.8 %copy.31 = bf16[32,4,2,2048]{3,0,2,1:T(8,128)(2,1)S(1)} copy(bf16[32,4,2,2048]{3,1,2,0:T(4,128)(2,1)} %all-gather.4.cloned.1.call-done) | data formatting | bytes 2097152 | tf_op jit(solution)/shard_map/while | solution.py:85
  55.9 13.3 %while.10 = (s32[]{:T(128)}, bf16[2,8,32,512]{3,2,1,0:T(8,128)(2,1)S(1)}, bf16[2,8,4]{1,2,0:T(4,128)(2,1)S(1)}, f32[32,4]{0,1:T(4,128)S(1)}, bf16[32,4,2,2048]{3...) while((s32[]{:T(128)}, ...), condition=%wide.region_2.3_spmd, body=%wide.region_1.2_spmd.sunk | while | flops 1099698688 | bytes 35148352 | solution.py:85
  55.9 0.2 multiply_multiply_fusion.5
  56.2 0.2 bitcast_convert_fusion.11
  56.4 0.0 copy-start
  56.4 2.3 %add_convert_fusion.5 = bf16[8,32,2048]{2,1,0:T(8,128)(2,1)S(1)} fusion(f32[8,2048]{1,0:T(8,128)S(1)} %get-tuple-element.186, f32[32,2048]{1,0:T(8,128)S(1)} %get-tuple-element.187, f32[8,2048]{1,0:T(8,128)S(1)} %get-tuple-element.188, f32[32,2048]{1,0:T(8,128)S(1)} %get-tuple-element.189, f32[8,32]{1,0:T(8,128)S(1)} %get-tuple-element.198, ...), kind=kLoop, calls=%fused_computation.6.clone.1 | loop fusion | flops 10485760 | bytes 3674112 | tf_op jit(solution)/shard_map/while/body/eval_jaxpr/convert_element_type | solution.py:66
  58.7 2.5 %add_convert_fusion.4 = bf16[8,32,2048]{2,1,0:T(8,128)(2,1)S(1)} fusion(f32[8,2048]{1,0:T(8,128)S(1)} %get-tuple-element.186, f32[32,2048]{1,0:T(8,128)S(1)} %get-tuple-element.187, f32[8,2048]{1,0:T(8,128)S(1)} %get-tuple-element.188, f32[32,2048]{1,0:T(8,128)S(1)} %get-tuple-element.189, f32[8,32]{1,0:T(8,128)S(1)} %get-tuple-element.198, ...), kind=kLoop, calls=%fused_computation.5.clone.1 | loop fusion | flops 10485760 | bytes 3674112 | tf_op jit(solution)/shard_map/while/body/eval_jaxpr/convert_element_type | solution.py:66
  61.2 0.0 copy-done
  61.2 1.2 %fusion.48 = bf16[2,8,32,512]{3,2,1,0:T(8,128)(2,1)S(1)} fusion(bf16[2,8,32,512]{3,2,1,0:T(8,128)(2,1)S(1)} %get-tuple-element.223, s32[]{:T(128)} %get-tuple-element.222, bf16[4096,512]{1,0:T(8,128)(2,1)S(1)} %copy-done, bf16[8,32,2048]{2,1,0:T(8,128)(2,1)S(1)} %add_convert_fusion.4, bf16[8,32,2048]{2,1,0:T(8,128)(2,1)S(1)} %add_convert_fusion.5), kind=kOutput, calls=%fused_computation.9.clone.1 | convolution fusion | flops 1078067200 | bytes 6553604 | tf_op jit(solution)/shard_map/while/body/eval_jaxpr/iqk,kl->iql/dot_general | solution.py:68
  62.5 0.2 multiply_multiply_fusion.5
  62.8 0.2 bitcast_convert_fusion.11
  63.1 0.0 copy-start
  63.1 2.3 %add_convert_fusion.5 = bf16[8,32,2048]{2,1,0:T(8,128)(2,1)S(1)} fusion(f32[8,2048]{1,0:T(8,128)S(1)} %get-tuple-element.186, f32[32,2048]{1,0:T(8,128)S(1)} %get-tuple-element.187, f32[8,2048]{1,0:T(8,128)S(1)} %get-tuple-element.188, f32[32,2048]{1,0:T(8,128)S(1)} %get-tuple-element.189, f32[8,32]{1,0:T(8,128)S(1)} %get-tuple-element.198, ...), kind=kLoop, calls=%fused_computation.6.clone.1 | loop fusion | flops 10485760 | bytes 3674112 | tf_op jit(solution)/shard_map/while/body/eval_jaxpr/convert_element_type | solution.py:66
  65.4 2.5 %add_convert_fusion.4 = bf16[8,32,2048]{2,1,0:T(8,128)(2,1)S(1)} fusion(f32[8,2048]{1,0:T(8,128)S(1)} %get-tuple-element.186, f32[32,2048]{1,0:T(8,128)S(1)} %get-tuple-element.187, f32[8,2048]{1,0:T(8,128)S(1)} %get-tuple-element.188, f32[32,2048]{1,0:T(8,128)S(1)} %get-tuple-element.189, f32[8,32]{1,0:T(8,128)S(1)} %get-tuple-element.198, ...), kind=kLoop, calls=%fused_computation.5.clone.1 | loop fusion | flops 10485760 | bytes 3674112 | tf_op jit(solution)/shard_map/while/body/eval_jaxpr/convert_element_type | solution.py:66
  67.9 0.0 copy-done
  67.9 1.2 %fusion.48 = bf16[2,8,32,512]{3,2,1,0:T(8,128)(2,1)S(1)} fusion(bf16[2,8,32,512]{3,2,1,0:T(8,128)(2,1)S(1)} %get-tuple-element.223, s32[]{:T(128)} %get-tuple-element.222, bf16[4096,512]{1,0:T(8,128)(2,1)S(1)} %copy-done, bf16[8,32,2048]{2,1,0:T(8,128)(2,1)S(1)} %add_convert_fusion.4, bf16[8,32,2048]{2,1,0:T(8,128)(2,1)S(1)} %add_convert_fusion.5), kind=kOutput, calls=%fused_computation.9.clone.1 | convolution fusion | flops 1078067200 | bytes 6553604 | tf_op jit(solution)/shard_map/while/body/eval_jaxpr/iqk,kl->iql/dot_general | solution.py:68
  69.1 0.0 copy-start.3
  69.1 0.8 %copy-done.3 = bf16[2,8,32,512]{3,2,1,0:T(8,128)(2,1)} copy-done((bf16[2,8,32,512]{3,2,1,0:T(8,128)(2,1)}, bf16[2,8,32,512]{3,2,1,0:T(8,128)(2,1)S(1)}, u32[]{:S(2)}) %copy-start.3) | copy-done | bytes 524312
  (15 shorter events, 0.3 us)
Async XLA Ops:
  6.5 2.2 %copy-start.1 = (bf16[4,4,2,2048]{3,2,1,0:T(2,128)(2,1)S(1)}, bf16[4,4,2,2048]{3,2,1,0:T(2,128)(2,1)}, u32[]{:S(2)}) copy-start(bf16[4,4,2,2048]{3,2,1,0:T(2,128)(2,1)} %param.4) | copy-start | bytes 393220
  6.5 47.5 %all-gather.4.cloned.1.call-start = ((), (), s32[]{:S(2)}) async-start(), calls=%async_computation | async-start | bytes 1179648 | tf_op jit(solution)/shard_map/all_gather | solution.py:97
  8.9 21.5 %collective-permute-start = (bf16[4,4,2,2048]{3,0,2,1:T(4,128)(2,1)S(1)}, bf16[4,4,2,2048]{3,0,2,1:T(4,128)(2,1)S(1)}, u32[]{:S(2)}, u32[]{:S(2)}) collective-permute-start(bf16[4,4,2,2048]{3,0,2,1:T(4,128)(2,1)S(1)} %multiply_convert_fusion.2), channel_id=1, source_target_pairs={{0,1},{1,0},{2,3},{3,2},{4,5},{5,4},{6,7},{7,6},{8,9},{9,8},{10,11... | collective-permute-start | bytes 393224 | tf_op jit(solution)/shard_map/ppermute | solution.py:17
  12.7 17.7 %copy-start.2 = (s32[4,4]{1,0:T(4,128)S(1)}, s32[4,4]{1,0:T(4,128)}, u32[]{:S(2)}) copy-start(s32[4,4]{1,0:T(4,128)} %param.5) | copy-start | bytes 196
  30.6 23.3 %collective-permute-start.1 = (bf16[8,4,2,2048]{3,0,2,1:T(8,128)(2,1)S(1)}, bf16[8,4,2,2048]{3,0,2,1:T(8,128)(2,1)S(1)}, u32[]{:S(2)}, u32[]{:S(2)}) collective-permute-start(bf16[8,4,2,2048]{3,0,2,1:T(8,128)(2,1)S(1)} %maximum_select_fusion.1), channel_id=1, source_target_pairs={{0,2},{1,3},{2,0},{3,1},{4,6},{5,7},{6,4},{7,5},{8,10},{9,11},{10,... | collective-permute-start | bytes 786440 | tf_op jit(solution)/shard_map/ppermute | solution.py:17
  56.4 4.8 %copy-start = (bf16[4096,512]{1,0:T(8,128)(2,1)S(1)}, bf16[4096,512]{1,0:T(8,128)(2,1)}, u32[]{:S(2)}) copy-start(bf16[4096,512]{1,0:T(8,128)(2,1)} %get-tuple-element.236) | copy-start | bytes 12582916 | tf_op jit(solution)/shard_map/while
  63.1 4.8 %copy-start = (bf16[4096,512]{1,0:T(8,128)(2,1)S(1)}, bf16[4096,512]{1,0:T(8,128)(2,1)}, u32[]{:S(2)}) copy-start(bf16[4096,512]{1,0:T(8,128)(2,1)} %get-tuple-element.236) | copy-start | bytes 12582916 | tf_op jit(solution)/shard_map/while
  69.1 0.8 %copy-start.3 = (bf16[2,8,32,512]{3,2,1,0:T(8,128)(2,1)}, bf16[2,8,32,512]{3,2,1,0:T(8,128)(2,1)S(1)}, u32[]{:S(2)}) copy-start(bf16[2,8,32,512]{3,2,1,0:T(8,128)(2,1)S(1)} %get-tuple-element.42) | copy-start | bytes 1572868
Sparse Core Ops, SparseCore 0:
  12.8 22.4 all-gather.3
